TPU v7x, 128 devices: a whole 4x4x4 slice. The times are simulated.
128 devices in a mesh: redist: 32 (over x, y, core), rep: 4 (over z).
Axes of the slice: x: 4, y: 4, z: 4, core: 2. Of those that a mesh axis runs over, the one named last changes fastest.
Arguments:
- amplitudes: bfloat16 [4, 128, 1024, 1024], P(None, ('redist', 'rep')), may hold values from -6 to 6
- integrals: bfloat16 [128, 1024, 2, 1024], P(None, 'redist'), may hold values from -0.046875 to 0.046875
- occ_irrep: int32 [128], replicated, may hold values from 0 to 7, as said below
- virt_irrep: int32 [1024], replicated, may hold values from 0 to 7, as said below
Outputs:
- cycle_term: float32 [4, 1024, 2, 1024], P(None, None, None, 'redist')
Inputs may be any that keep to these rules, and one draw needn't show every extreme that they name: `occ_irrep`: labels never fall along the orbitals; each of the 8 irreps holds one contiguous range of between n // 16 and 3 * n // 16 orbitals, n being 128 or 1024. `virt_irrep`: labels never fall along the orbitals; each of the 8 irreps holds one contiguous range of between n // 16 and 3 * n // 16 orbitals, n being 128 or 1024.
All inputs are finite; a program needn't handle non-finite values.
Results may differ from a plain program's by a relative error of at most 0.0003.
Values may be sent and summed in bfloat16 or wider, within the bound.
No kernel may reach another device: no remote copies, remote signals or barrier semaphores. Data moves between devices by JAX's collectives and lax.ppermute only.
A program may use at most 192 MiB of HBM per device.

v0:
```python
import jax
import jax.numpy as jnp
from jax import lax
from jax.sharding import PartitionSpec as P

N_IRREPS = 8


def irrep_windows(virt_irrep, width):
    count = virt_irrep.shape[0]
    starts = jnp.sum(
        (virt_irrep[None, :] < jnp.arange(N_IRREPS, dtype=virt_irrep.dtype)[:, None]).astype(
            jnp.int32
        ),
        axis=1,
    )
    return jnp.minimum(starts, count - width)


def parts_in(span, count):
    return min(N_IRREPS, -(-span // (count // 16)) + 1)


def body(amplitudes, integrals, occ_irrep, virt_irrep):
    n_redist = lax.axis_size("redist")
    n_rep = lax.axis_size("rep")
    dev_index = lax.axis_index("redist")
    rep_index = lax.axis_index("rep")
    i_slab, k_block, v_width, _ = amplitudes.shape
    c_block = integrals.shape[1]
    j_slab = integrals.shape[2]
    width = 3 * v_width // 16
    wins = irrep_windows(virt_irrep, width)
    occ_rows = occ_irrep[:i_slab]
    occ_js = occ_irrep[:j_slab]
    grouped = integrals.reshape(n_redist, n_rep, k_block, c_block, j_slab, v_width)
    mine = lax.dynamic_index_in_dim(grouped, rep_index, 1, keepdims=False)
    mine = mine.reshape(n_redist * k_block, c_block, j_slab, v_width)
    dest_k = (
        (jnp.arange(n_redist, dtype=jnp.int32)[:, None] * n_rep + rep_index) * k_block
        + jnp.arange(k_block, dtype=jnp.int32)[None, :]
    ).reshape(-1)
    dest_lab = occ_irrep[dest_k]
    c_lab = lax.dynamic_slice_in_dim(virt_irrep, dev_index * c_block, c_block)
    n_cparts = parts_in(c_block, v_width)
    pieces = []
    for d in range(n_redist * k_block):
        row = mine[d]
        piece = jnp.zeros((c_block, j_slab, width), integrals.dtype)
        for p in range(n_cparts):
            lab = jnp.minimum(c_lab[0] + p, N_IRREPS - 1)
            start = wins[jnp.bitwise_xor(lab, dest_lab[d])]
            cut = lax.dynamic_slice_in_dim(row, start, width, axis=2)
            piece = jnp.where((c_lab == c_lab[0] + p)[:, None, None], cut, piece)
        pieces.append(piece)
    packed = jnp.stack(pieces)
    moved = lax.all_to_all(packed, "redist", split_axis=0, concat_axis=1, tiled=True)
    moved = moved.reshape(k_block, n_redist * c_block, j_slab, width)
    my_k0 = (dev_index * n_rep + rep_index) * k_block
    blocks = []
    for kk in range(k_block):
        k_lab = occ_irrep[my_k0 + kk]
        amp = amplitudes[:, kk]
        ints = moved[kk]
        pair_ik = jnp.bitwise_xor(occ_rows, k_lab)
        per_g = []
        for g in range(N_IRREPS):
            c_irrep = jnp.bitwise_xor(g, k_lab)
            wa = wins[g]
            wc = wins[c_irrep]
            a_lab = lax.dynamic_slice_in_dim(virt_irrep, wa, width)
            cw_lab = lax.dynamic_slice_in_dim(virt_irrep, wc, width)
            a_blk = lax.dynamic_slice(amp, (0, wa, wc), (i_slab, width, width))
            allowed = (
                pair_ik[:, None, None] == jnp.bitwise_xor(a_lab[:, None], cw_lab[None, :])[None]
            )
            a_blk = jnp.where(allowed, a_blk, jnp.zeros((), a_blk.dtype))
            i_blk = lax.dynamic_slice_in_dim(ints, wc, width, axis=0)
            sym = (cw_lab == c_irrep)[:, None, None] & (
                jnp.bitwise_xor(cw_lab, k_lab)[:, None, None]
                == jnp.bitwise_xor(occ_js[:, None], a_lab[None, :])[None]
            )
            i_blk = jnp.where(sym, i_blk, jnp.zeros((), i_blk.dtype))
            blk = lax.dot_general(
                i_blk, a_blk, (((0,), (2,)), ((), ())), preferred_element_type=jnp.float32
            )
            per_g.append(jnp.transpose(blk, (1, 0, 2, 3)).reshape(width, -1))
        blocks.append(jnp.concatenate(per_g, axis=0))
    every = blocks[0]
    for more in blocks[1:]:
        every = every + more
    b_pos = jnp.arange(v_width, dtype=jnp.int32)
    pick = virt_irrep * width + (b_pos - wins[virt_irrep])
    compact = jnp.take(every, pick, axis=0)
    shares = lax.psum_scatter(compact, ("redist", "rep"), scatter_dimension=0, tiled=True)
    mine_b = lax.all_gather(shares, "rep", axis=0, tiled=True)
    nb = mine_b.shape[0]
    b_lab = lax.dynamic_slice_in_dim(virt_irrep, dev_index * nb, nb)
    vals = mine_b.reshape(nb, j_slab, i_slab, width).transpose(2, 3, 1, 0)
    out = jnp.zeros((i_slab, v_width, j_slab, nb), jnp.float32)
    for p in range(parts_in(nb, v_width)):
        lab = b_lab[0] + p
        part = jnp.where((b_lab == lab)[None, None, None, :], vals, 0.0)
        start = wins[jnp.minimum(lab, N_IRREPS - 1)]
        placed = lax.dynamic_update_slice(
            jnp.zeros((i_slab, v_width, j_slab, nb), jnp.float32), part, (0, start, 0, 0)
        )
        out = out + placed
    return out


def solution(mesh):
    placed = (P(None, ("redist", "rep"), None, None), P(None, "redist", None, None), P(), P())
    return jax.shard_map(
        body, mesh=mesh, in_specs=placed, out_specs=P(None, None, None, "redist"), check_vma=False
    )
```

profile of v0, /device:TPU:0, one launch (start us, length us, event | category | flops | bytes accessed | tf_op | source)
XLA Modules:
  0.0 598.9 jit_solution(7848239957368478515)
XLA Ops:
  6.6 1.4 gather_fusion
  15.3 1.3 dynamic_slice.666
  144.4 16.4 %copy.38 = bf16[128,32,2,1024]{3,1,2,0:T(8,128)(2,1)} copy(bf16[128,32,2,1024]{3,2,1,0:T(2,128)(2,1)} %param.5) | data formatting | bytes 33554432 | tf_op args[1]
  200.8 1.6 constant_dynamic-update-slice_fusion.31
  202.4 1.6 constant_dynamic-update-slice_fusion.30
  203.9 1.6 constant_dynamic-update-slice_fusion.29
  205.5 1.6 constant_dynamic-update-slice_fusion.28
  207.1 1.6 constant_dynamic-update-slice_fusion.27
  208.7 1.6 constant_dynamic-update-slice_fusion.26
  210.3 1.6 constant_dynamic-update-slice_fusion.25
  211.9 1.6 constant_dynamic-update-slice_fusion.24
  213.5 1.6 constant_dynamic-update-slice_fusion.23
  215.0 1.6 constant_dynamic-update-slice_fusion.22
  216.6 1.6 constant_dynamic-update-slice_fusion.21
  218.2 1.6 constant_dynamic-update-slice_fusion.20
  219.8 1.6 constant_dynamic-update-slice_fusion.19
  221.4 1.6 constant_dynamic-update-slice_fusion.18
  223.0 1.6 constant_dynamic-update-slice_fusion.17
  224.5 1.6 constant_dynamic-update-slice_fusion.16
  226.1 1.6 constant_dynamic-update-slice_fusion.15
  227.7 1.6 constant_dynamic-update-slice_fusion.14
  229.3 1.6 constant_dynamic-update-slice_fusion.13
  230.9 1.6 constant_dynamic-update-slice_fusion.12
  232.5 1.6 constant_dynamic-update-slice_fusion.11
  234.0 1.6 constant_dynamic-update-slice_fusion.10
  235.6 1.6 constant_dynamic-update-slice_fusion.9
  237.2 1.6 constant_dynamic-update-slice_fusion.8
  238.8 1.6 constant_dynamic-update-slice_fusion.7
  240.4 1.6 constant_dynamic-update-slice_fusion.6
  242.0 1.6 constant_dynamic-update-slice_fusion.5
  243.6 1.6 constant_dynamic-update-slice_fusion.4
  245.1 1.5 constant_dynamic-update-slice_fusion.3
  246.7 1.5 constant_dynamic-update-slice_fusion.2
  248.2 1.5 constant_dynamic-update-slice_fusion.1
  249.8 1.6 constant_dynamic-update-slice_fusion
  251.3 7.1 %all-to-all-start = ((bf16[32,32,2,192]{3,1,2,0:T(8,128)(2,1)}), bf16[32,32,2,192]{3,1,2,0:T(8,128)(2,1)S(1)}, u32[]{:S(2)}, u32[]{:S(2)}) async-start(bf16[32,32,2,192]{3,1,2,0:T(8,128)(2,1)} %constant_dynamic-update-slice_fusion), calls=%async_computation | async-start | bytes 2097152 | tf_op jit(solution)/shard_map/all_to_all | solution.py:57
  278.6 4.9 compare_and_fusion
  300.6 1.7 fusion.4
  302.3 1.5 copy.41
  303.7 1.6 fusion.1
  305.4 1.5 copy.40
  306.9 2.4 constant_dynamic-update-slice_fusion.39
  309.3 1.7 fusion.7
  310.9 1.5 copy.42
  312.4 1.7 fusion.10
  314.1 1.5 copy.43
  315.6 1.6 fusion.13
  317.2 1.5 copy.44
  318.7 1.6 fusion.16
  320.3 1.5 copy.45
  321.9 1.6 fusion.19
  323.5 1.5 copy.46
  325.0 1.5 fusion.22
  326.5 1.5 copy.47
  328.0 2.5 constant_dynamic-update-slice_fusion.38
  330.5 2.4 constant_dynamic-update-slice_fusion.37
  332.9 2.4 constant_dynamic-update-slice_fusion.36
  335.3 2.4 constant_dynamic-update-slice_fusion.35
  340.0 1.2 constant_dynamic-update-slice_fusion.32
  341.2 11.4 %gather_fusion.1 = f32[1024,1536]{1,0:T(8,128)} fusion(f32[1536,1536]{1,0:T(8,128)} %constant_dynamic-update-slice_fusion.32, s32[1024]{0:T(1024)S(1)} %broadcast_clamp_fusion), kind=kCustom, calls=%fused_computation.1 | custom fusion | bytes 12587008 | tf_op jit(solution)/shard_map/jit(_take)/gather | solution.py:94
  352.6 5.9 broadcast_select_fusion
  362.5 212.3 %reduce-scatter.2.cloned.1.call-done = f32[8,1536]{1,0:T(8,128)} async-done(((f32[1024,1536]{1,0:T(8,128)}), f32[8,1536]{1,0:T(8,128)}) %reduce-scatter.2.cloned.1.call-update) | async-done | bytes 49168 | tf_op jit(solution)/shard_map/reduce_scatter | solution.py:95
  574.7 12.3 %all_gather.3 = f32[32,1536]{1,0:T(8,128)S(1)} all-gather(f32[8,1536]{1,0:T(8,128)} %reduce-scatter.2.cloned.1.call-done), channel_id=1, replica_groups=mesh['redist'=32,'rep'=4] {'rep'}, dimensions={0}, use_global_device_ids=true | all-gather | bytes 245760 | tf_op jit(solution)/shard_map/all_gather | solution.py:96
  589.0 3.0 add.795
  (51 shorter events, 19.3 us)
Async XLA Ops:
  144.4 134.2 %copy-start.6 = (s32[1024]{0:T(1024)S(1)}, s32[1024]{0:T(1024)}, u32[]{:S(2)}) copy-start(s32[1024]{0:T(1024)} %param.7) | copy-start | bytes 12292
  144.4 153.6 %copy-start = (s32[128]{0:T(128)S(1)}, s32[128]{0:T(128)}, u32[]{:S(2)}) copy-start(s32[128]{0:T(128)} %param.6) | copy-start | bytes 1540
  251.3 49.2 %all-to-all-start = ((bf16[32,32,2,192]{3,1,2,0:T(8,128)(2,1)}), bf16[32,32,2,192]{3,1,2,0:T(8,128)(2,1)S(1)}, u32[]{:S(2)}, u32[]{:S(2)}) async-start(bf16[32,32,2,192]{3,1,2,0:T(8,128)(2,1)} %constant_dynamic-update-slice_fusion), calls=%async_computation | async-start | bytes 2097152 | tf_op jit(solution)/shard_map/all_to_all | solution.py:57
  258.4 316.3 %reduce-scatter.2.cloned.1.call-start = ((), (), s32[]{:S(2)}) async-start(), calls=%async_computation.2 | async-start | bytes 6340608 | tf_op jit(solution)/shard_map/reduce_scatter | solution.py:95
  305.4 10.2 %copy-start.5 = (s32[192,192]{1,0:T(8,128)S(1)}, s32[192,192]{1,0:T(8,128)}, u32[]{:S(2)}) copy-start(s32[192,192]{1,0:T(8,128)} %get-tuple-element.180) | copy-start | bytes 442372
  328.0 9.7 %copy-start.1 = (f32[192,1536]{1,0:T(8,128)S(1)}, f32[192,1536]{1,0:T(8,128)}, u32[]{:S(2)}) copy-start(f32[192,1536]{1,0:T(8,128)} %copy.45) | copy-start | bytes 3538948
  328.0 10.8 %copy-start.2 = (f32[192,1536]{1,0:T(8,128)S(1)}, f32[192,1536]{1,0:T(8,128)}, u32[]{:S(2)}) copy-start(f32[192,1536]{1,0:T(8,128)} %copy.46) | copy-start | bytes 3538948
  328.0 11.9 %copy-start.3 = (f32[192,1536]{1,0:T(8,128)S(1)}, f32[192,1536]{1,0:T(8,128)}, u32[]{:S(2)}) copy-start(f32[192,1536]{1,0:T(8,128)} %copy.47) | copy-start | bytes 3538948
  588.1 1.0 copy-start.4
Sparse Core Ops, SparseCore 0:
  358.7 216.0 reduce-scatter.1
where the time goes:
time: 605 us; the launch traced here: 599 us
  between operations  215 us (36%)
  waiting for transfers between devices  212 us (35%)
  other arithmetic  70.2 us (12%)
  local copies, waits for them, and re-layouts  69 us (11%)
  matrix products  13 us (2%)
  blocking collectives  12.3 us (2%)
  starting transfers between devices  7.32 us (1%)
    reduce_scatter x1, waiting for transfers between devices, body(): lax.psum_scatter(compact, ('redist', 'rep'), scatter_dimension=0, tiled=T...  212 us
    unnamed x31, other arithmetic  49 us
    unnamed x22, local copies, waits for them, and re-layouts  31.6 us
    dot_general x8, matrix products, body(): lax.dot_general(i_blk, a_blk, (((0,), (2,)), ((), ())), preferred_element...  13 us
    all_gather x1, blocking collectives, body(): mine_b = lax.all_gather(shares, 'rep', axis=0, tiled=True)  12.3 us
  transfers between devices with their start and end apart: 2, of which 1 were waited for; matrix products, arithmetic and copies ran while one was open for 2% of the time, Pallas kernels for 0%

commit v1 on v0

--- a/solution.py
+++ b/solution.py
@@ -93,7 +93,8 @@
     pick = virt_irrep * width + (b_pos - wins[virt_irrep])
     compact = jnp.take(every, pick, axis=0)
     shares = lax.psum_scatter(compact, ("redist", "rep"), scatter_dimension=0, tiled=True)
-    mine_b = lax.all_gather(shares, "rep", axis=0, tiled=True)
+    outgoing = jnp.stack([shares] * lax.axis_size("rep"))
+    mine_b = jnp.concatenate(lax.all_to_all(outgoing, "rep", 0, 0), axis=0)
     nb = mine_b.shape[0]
     b_lab = lax.dynamic_slice_in_dim(virt_irrep, dev_index * nb, nb)
     vals = mine_b.reshape(nb, j_slab, i_slab, width).transpose(2, 3, 1, 0)

time: 605 us -> 622 us (1.028)
  the two profiles are of different devices: /device:TPU:0 before, /device:TPU:2 now
where the time goes in v1:
time: 622 us; the launch traced here: 616 us
  waiting for transfers between devices  217 us (35%)
  between operations  215 us (35%)
  local copies, waits for them, and re-layouts  90 us (14%)
  other arithmetic  70.2 us (11%)
  matrix products  13 us (2%)
  starting transfers between devices  11.4 us (2%)
    reduce_scatter x1, waiting for transfers between devices, body(): lax.psum_scatter(compact, ('redist', 'rep'), scatter_dimension=0, tiled=T...  215 us
    unnamed x31, other arithmetic  48.6 us
    unnamed x20, local copies, waits for them, and re-layouts  30.8 us
    dot_general x8, matrix products, body(): lax.dot_general(i_blk, a_blk, (((0,), (2,)), ((), ())), preferred_element...  13 us
    add x2, local copies, waits for them, and re-layouts, body(): out = out + placed  12.7 us
  transfers between devices with their start and end apart: 3, of which 2 were waited for; matrix products, arithmetic and copies ran while one was open for 2% of the time, Pallas kernels for 0%

profile of v1, /device:TPU:2, one launch (start us, length us, event | category | flops | bytes accessed | tf_op | source)
XLA Modules:
  0.0 616.1 jit_solution(8289112720962594651)
XLA Ops:
  144.0 16.5 %copy.34 = bf16[128,32,2,1024]{3,1,2,0:T(8,128)(2,1)} copy(bf16[128,32,2,1024]{3,2,1,0:T(2,128)(2,1)} %param.5) | data formatting | bytes 33554432 | tf_op args[1]
  200.2 1.6 constant_dynamic-update-slice_fusion.31
  201.8 1.6 constant_dynamic-update-slice_fusion.30
  203.4 1.6 constant_dynamic-update-slice_fusion.29
  205.0 1.6 constant_dynamic-update-slice_fusion.28
  206.5 1.6 constant_dynamic-update-slice_fusion.27
  208.1 1.6 constant_dynamic-update-slice_fusion.26
  209.7 1.6 constant_dynamic-update-slice_fusion.25
  211.3 1.6 constant_dynamic-update-slice_fusion.24
  212.9 1.6 constant_dynamic-update-slice_fusion.23
  214.5 1.6 constant_dynamic-update-slice_fusion.22
  216.1 1.6 constant_dynamic-update-slice_fusion.21
  217.6 1.6 constant_dynamic-update-slice_fusion.20
  219.2 1.6 constant_dynamic-update-slice_fusion.19
  220.8 1.6 constant_dynamic-update-slice_fusion.18
  222.4 1.6 constant_dynamic-update-slice_fusion.17
  224.0 1.6 constant_dynamic-update-slice_fusion.16
  225.6 1.6 constant_dynamic-update-slice_fusion.15
  227.2 1.6 constant_dynamic-update-slice_fusion.14
  228.7 1.6 constant_dynamic-update-slice_fusion.13
  230.3 1.6 constant_dynamic-update-slice_fusion.12
  231.9 1.5 constant_dynamic-update-slice_fusion.11
  233.4 1.5 constant_dynamic-update-slice_fusion.10
  235.0 1.5 constant_dynamic-update-slice_fusion.9
  236.5 1.5 constant_dynamic-update-slice_fusion.8
  238.0 1.5 constant_dynamic-update-slice_fusion.7
  239.6 1.5 constant_dynamic-update-slice_fusion.6
  241.1 1.5 constant_dynamic-update-slice_fusion.5
  242.6 1.5 constant_dynamic-update-slice_fusion.4
  244.1 1.6 constant_dynamic-update-slice_fusion.3
  245.7 1.6 constant_dynamic-update-slice_fusion.2
  247.3 1.6 constant_dynamic-update-slice_fusion.1
  248.8 1.6 constant_dynamic-update-slice_fusion
  250.4 7.6 %all-to-all-start = ((bf16[32,32,2,192]{3,1,2,0:T(8,128)(2,1)}), bf16[32,32,2,192]{3,1,2,0:T(8,128)(2,1)S(1)}, u32[]{:S(2)}, u32[]{:S(2)}) async-start(bf16[32,32,2,192]{3,1,2,0:T(8,128)(2,1)} %constant_dynamic-update-slice_fusion), calls=%async_computation | async-start | bytes 2097152 | tf_op jit(solution)/shard_map/all_to_all | solution.py:57
  278.5 5.2 compare_and_fusion
  300.9 1.7 fusion.4
  302.6 1.5 copy.37
  304.1 1.6 fusion.1
  305.7 1.5 copy.36
  307.2 2.4 constant_dynamic-update-slice_fusion.39
  309.6 1.7 fusion.7
  311.3 1.5 copy.38
  312.7 1.6 fusion.10
  315.9 1.6 fusion.13
  317.5 1.5 copy.40
  319.0 1.6 fusion.16
  320.6 1.5 copy.41
  322.2 1.5 fusion.19
  323.7 1.5 copy.42
  325.2 1.6 fusion.22
  326.8 1.5 copy.43
  328.3 2.5 constant_dynamic-update-slice_fusion.38
  330.8 2.4 constant_dynamic-update-slice_fusion.37
  333.2 2.4 constant_dynamic-update-slice_fusion.36
  335.6 2.4 constant_dynamic-update-slice_fusion.35
  341.5 11.4 %gather_fusion.1 = f32[1024,1536]{1,0:T(8,128)} fusion(f32[1536,1536]{1,0:T(8,128)} %constant_dynamic-update-slice_fusion.32, s32[1024]{0:T(1024)S(1)} %broadcast_clamp_fusion), kind=kCustom, calls=%fused_computation.1 | custom fusion | bytes 12587008 | tf_op jit(solution)/shard_map/jit(_take)/gather | solution.py:94
  352.9 5.9 broadcast_select_fusion
  358.8 214.6 %reduce-scatter.2.cloned.1.call-done = f32[8,1536]{1,0:T(8,128)} async-done(((f32[1024,1536]{1,0:T(8,128)}), f32[8,1536]{1,0:T(8,128)}) %reduce-scatter.2.cloned.1.call-update) | async-done | bytes 49168 | tf_op jit(solution)/shard_map/reduce_scatter | solution.py:95
  573.5 1.5 stack.5
  574.9 3.6 all-to-all-start.1
  582.3 2.3 all-to-all-done.1
  585.2 11.1 %dynamic_update_slice.8 = f32[4,1024,2,32]{1,0,2,3:T(4,128)S(1)} dynamic-update-slice(f32[4,1024,2,32]{1,0,2,3:T(4,128)S(1)} %broadcast.1051, f32[4,192,2,32]{1,0,2,3:T(4,128)S(1)} %select_bitcast_fusion, s32[]{:T(128)} %constant.121.clone.1, s32[]{:T(128)S(6)} %select_n.1471, s32[]{:T(128)} %constant.121.clone.1, s32[]{:T(128)} %constant.121.clone.1) | dynamic-update-slice | bytes 393220 | tf_op jit(solution)/shard_map/dynamic_update_slice | solution.py:106
  596.6 11.1 %add.795 = f32[4,1024,2,32]{1,0,2,3:T(4,128)S(1)} dynamic-update-slice(f32[4,1024,2,32]{1,0,2,3:T(4,128)S(1)} %dynamic_update_slice.8, f32[4,192,2,32]{1,0,2,3:T(4,128)S(1)} %bitcast_add_fusion, s32[]{:T(128)} %constant.121.clone.1, s32[]{:T(128)S(6)} %select_n.1473, s32[]{:T(128)} %constant.121.clone.1, s32[]{:T(128)} %constant.121.clone.1) | dynamic-update-slice | bytes 393220 | tf_op jit(solution)/shard_map/add | solution.py:109
  607.7 1.6 copy.44
  (52 shorter events, 23.4 us)
Async XLA Ops:
  143.9 134.5 %copy-start.5 = (s32[1024]{0:T(1024)S(1)}, s32[1024]{0:T(1024)}, u32[]{:S(2)}) copy-start(s32[1024]{0:T(1024)} %param.7) | copy-start | bytes 12292
  144.0 154.3 %copy-start = (s32[128]{0:T(128)S(1)}, s32[128]{0:T(128)}, u32[]{:S(2)}) copy-start(s32[128]{0:T(128)} %param.6) | copy-start | bytes 1540
  250.4 50.4 %all-to-all-start = ((bf16[32,32,2,192]{3,1,2,0:T(8,128)(2,1)}), bf16[32,32,2,192]{3,1,2,0:T(8,128)(2,1)S(1)}, u32[]{:S(2)}, u32[]{:S(2)}) async-start(bf16[32,32,2,192]{3,1,2,0:T(8,128)(2,1)} %constant_dynamic-update-slice_fusion), calls=%async_computation | async-start | bytes 2097152 | tf_op jit(solution)/shard_map/all_to_all | solution.py:57
  258.1 315.4 %reduce-scatter.2.cloned.1.call-start = ((), (), s32[]{:S(2)}) async-start(), calls=%async_computation.3 | async-start | bytes 6340608 | tf_op jit(solution)/shard_map/reduce_scatter | solution.py:95
  305.7 10.2 %copy-start.4 = (s32[192,192]{1,0:T(8,128)S(1)}, s32[192,192]{1,0:T(8,128)}, u32[]{:S(2)}) copy-start(s32[192,192]{1,0:T(8,128)} %get-tuple-element.180) | copy-start | bytes 442372
  328.3 9.6 %copy-start.1 = (f32[192,1536]{1,0:T(8,128)S(1)}, f32[192,1536]{1,0:T(8,128)}, u32[]{:S(2)}) copy-start(f32[192,1536]{1,0:T(8,128)} %copy.41) | copy-start | bytes 3538948
  328.3 10.8 %copy-start.2 = (f32[192,1536]{1,0:T(8,128)S(1)}, f32[192,1536]{1,0:T(8,128)}, u32[]{:S(2)}) copy-start(f32[192,1536]{1,0:T(8,128)} %copy.42) | copy-start | bytes 3538948
  328.3 11.9 %copy-start.3 = (f32[192,1536]{1,0:T(8,128)S(1)}, f32[192,1536]{1,0:T(8,128)}, u32[]{:S(2)}) copy-start(f32[192,1536]{1,0:T(8,128)} %copy.43) | copy-start | bytes 3538948
  574.9 9.7 %all-to-all-start.1 = ((f32[4,8,1536]{2,1,0:T(8,128)}), f32[4,8,1536]{2,1,0:T(8,128)S(1)}, u32[]{:S(2)}, u32[]{:S(2)}) async-start(f32[4,8,1536]{2,1,0:T(8,128)} %stack.5), calls=%async_computation.2 | async-start | bytes 393216 | tf_op jit(solution)/shard_map/all_to_all | solution.py:97
Sparse Core Ops, SparseCore 0:
  359.0 214.4 reduce-scatter.1
